TPU v7x, 32 devices: a whole 2x2x4 slice. The times are simulated.
32 devices in a mesh: row: 4 (over y, core), col: 8 (over z, x).
Axes of the slice: x: 2, y: 2, z: 4, core: 2. Of those that a mesh axis runs over, the one named last changes fastest.
Arguments:
- node_feats: bfloat16 [8192, 256], P(('row', 'col')), may hold values from -6 to 6
- weight: bfloat16 [256, 256], replicated, may hold values from -0.375 to 0.375
- cotangent: bfloat16 [8192, 256], P(('row', 'col')), may hold values from -6 to 6
- band_tiles: bfloat16 [384, 128, 128], P(('row', 'col')), may hold values from 0 to 0.049804688
- band_coords: int32 [384, 2], P(('row', 'col')), may hold values from 0 to 5, as said below
- bound_tiles: bfloat16 [1280, 128, 128], P(('row', 'col')), may hold values from 0 to 0.049804688
- bound_coords: int32 [1280, 2], P(('row', 'col')), may hold values from 0 to 7, as said below
- bound_count: int32 [32], P(('row', 'col')), may hold values from 0 to 40, as said below
- recv_lists: int32 [32, 8], P(('row', 'col')), may hold values from -1 to 1, as said below
- send_lists: int32 [32, 8], P(('row', 'col')), may hold values from -1 to 1, as said below
- reorder: int32 [32, 256], P(('row', 'col')), may hold values from 0 to 255, each once within a row
Outputs:
- node_out: bfloat16 [8192, 256], P(('row', 'col'))
- feat_grad: bfloat16 [8192, 256], P(('row', 'col'))
- weight_grad: float32 [256, 256], replicated
Inputs may be any that keep to these rules, and one draw needn't show every extreme that they name: recv_lists[r * 8 + c, s] is a row block of device r * 8 + s, below 2, or -1 for none; it is -1 where s = c. In every row group one device receives a block from every other column. send_lists[r * 8 + s, c] equals recv_lists[r * 8 + c, s]. bound_count[d] is at least the number of entries of recv_lists[d] that are not -1; in every row group one device has all 40 slots live. `bound_coords`: pairs (row block below 2, owner column below 8); for k < bound_count[d] the owner column s of slot k has recv_lists[d, s] >= 0, and every such column is named by one of them; slots from bound_count[d] on are not used. `band_coords`: pairs (row block below 2, extended column block below (768) / 128); no pair twice on one device. `reorder`: each row is a permutation.
All inputs are finite; a program needn't handle non-finite values.
Results may differ from a plain program's by a relative error of at most 0.0095.
Values may be sent and summed in bfloat16 or wider, within the bound.
No kernel may reach another device: no remote copies, remote signals or barrier semaphores. Data moves between devices by JAX's collectives and lax.ppermute only.
A program may use at most 64 MiB of HBM per device.

v0:
```python
import jax
import jax.numpy as jnp
from jax import lax
from jax.sharding import PartitionSpec as P

BW = 256


def padded_2(cells, sides, width):
    for axis, dim in sides:
        count = lax.axis_size(axis)
        head = lax.slice_in_dim(cells, 0, width, axis=dim)
        tail = lax.slice_in_dim(cells, cells.shape[dim] - width, cells.shape[dim], axis=dim)
        cells = jnp.concatenate(
            [
                lax.ppermute(tail, axis, [(i, (i + 1) % count) for i in range(count)]),
                cells,
                lax.ppermute(head, axis, [((i + 1) % count, i) for i in range(count)]),
            ],
            axis=dim,
        )
    return cells


def split_sum(selector, terms):
    high_part = terms.astype(jnp.bfloat16)
    low_part = (terms - high_part.astype(jnp.float32)).astype(jnp.bfloat16)
    pick = selector.astype(jnp.bfloat16)
    upper_sum = jnp.einsum("rk,kaf->raf", pick, high_part, preferred_element_type=jnp.float32)
    lower_sum = jnp.einsum("rk,kaf->raf", pick, low_part, preferred_element_type=jnp.float32)
    return upper_sum + lower_sum


def on_device(
    node_feats,
    weight,
    cotangent,
    band_tiles,
    band_coords,
    bound_tiles,
    bound_coords,
    bound_count,
    recv_lists,
    send_lists,
    reorder,
):
    tile_size = band_tiles.shape[1]
    row_count = node_feats.shape[0]
    width_feat = node_feats.shape[1]
    tile_rows = row_count // tile_size
    rim_tiles = BW // tile_size
    col_tiles = tile_rows + 2 * rim_tiles
    ext_count = row_count + 2 * BW
    peers = lax.axis_size("col")
    slot_total = bound_tiles.shape[0]
    order = reorder[0]
    inverse = (
        jnp.zeros((row_count,), jnp.int32).at[order].set(jnp.arange(row_count, dtype=jnp.int32))
    )
    x_band = jnp.take(node_feats, order, axis=0)
    hidden = jnp.dot(x_band, weight, preferred_element_type=jnp.float32).astype(jnp.bfloat16)
    band_row_ids = band_coords[:, 0]
    band_col_ids = band_coords[:, 1]
    band_dense = jnp.zeros((tile_rows, tile_size, col_tiles, tile_size), jnp.bfloat16)
    band_dense = (
        band_dense.at[band_row_ids, :, band_col_ids].set(band_tiles).reshape(row_count, ext_count)
    )
    extended = padded_2(hidden, (("row", 0),), BW)
    mixed = jnp.dot(band_dense, extended, preferred_element_type=jnp.float32)
    blocks = hidden.reshape(tile_rows, tile_size, width_feat)
    giving = send_lists[0]
    outgoing = jnp.where(
        (giving >= 0)[:, None, None],
        jnp.take(blocks, jnp.maximum(giving, 0), axis=0),
        jnp.zeros((), jnp.bfloat16),
    )
    arrived = lax.all_to_all(outgoing, "col", split_axis=0, concat_axis=0, tiled=True)
    tile_range = jnp.arange(tile_rows, dtype=jnp.int32)
    live_slots = jnp.arange(slot_total, dtype=jnp.int32) < bound_count[0]
    bound_row_ids = bound_coords[:, 0]
    bound_owner = bound_coords[:, 1]
    bound_onehot = (bound_row_ids[None, :] == tile_range[:, None]) & live_slots[None, :]
    slot_rows = jnp.take(arrived, bound_owner, axis=0).reshape(slot_total * tile_size, width_feat)
    placed = jnp.einsum(
        "rk,kab->rakb",
        bound_onehot.astype(jnp.bfloat16),
        bound_tiles,
        preferred_element_type=jnp.bfloat16,
    )
    placed = placed.reshape(row_count, slot_total * tile_size)
    mixed = mixed + jnp.dot(placed, slot_rows, preferred_element_type=jnp.float32)
    out_band = jax.nn.silu(mixed).astype(jnp.bfloat16)
    node_out = jnp.take(out_band, inverse, axis=0)
    grad_band = jnp.take(cotangent, order, axis=0).astype(jnp.float32)
    sigma = jax.nn.sigmoid(mixed)
    slope = (grad_band * sigma * (1.0 + mixed * (1.0 - sigma))).astype(jnp.bfloat16)
    slope_blocks = slope.reshape(tile_rows, tile_size, width_feat)
    ext_grad = lax.dot_general(
        band_dense, slope, (((0,), (0,)), ((), ())), preferred_element_type=jnp.float32
    )
    rim_terms = jnp.concatenate([ext_grad[:BW], ext_grad[BW + row_count :]], axis=0).astype(
        jnp.bfloat16
    )
    padded = padded_2(rim_terms, (("row", 0),), BW)
    grad_hidden = ext_grad[BW : BW + row_count]
    grad_hidden = grad_hidden.at[:BW].add(padded[:BW].astype(jnp.float32))
    grad_hidden = grad_hidden.at[row_count - BW :].add(padded[3 * BW :].astype(jnp.float32))
    slot_back = jnp.einsum(
        "kab,kaf->kbf",
        bound_tiles,
        jnp.take(slope_blocks, bound_row_ids, axis=0),
        preferred_element_type=jnp.float32,
    )
    owner_range = jnp.arange(peers, dtype=jnp.int32)
    owner_onehot = (bound_owner[None, :] == owner_range[:, None]) & live_slots[None, :]
    to_owner = split_sum(owner_onehot, slot_back).astype(jnp.bfloat16)
    returned = lax.all_to_all(to_owner, "col", split_axis=0, concat_axis=0, tiled=True)
    block_onehot = (giving[None, :] == tile_range[:, None]).astype(jnp.bfloat16)
    from_peers = jnp.einsum(
        "bs,saf->baf", block_onehot, returned, preferred_element_type=jnp.float32
    )
    grad_hidden = grad_hidden + from_peers.reshape(row_count, width_feat)
    grad_round = grad_hidden.astype(jnp.bfloat16)
    partial_weight = lax.dot_general(
        x_band, grad_round, (((0,), (0,)), ((), ())), preferred_element_type=jnp.float32
    )
    nodes_all = row_count * lax.axis_size("row") * peers
    weight_grad = lax.psum(partial_weight, ("row", "col")) * nodes_all ** (-0.5)
    feat_band = lax.dot_general(
        grad_round, weight, (((1,), (1,)), ((), ())), preferred_element_type=jnp.float32
    ).astype(jnp.bfloat16)
    feat_grad = jnp.take(feat_band, inverse, axis=0)
    return (node_out, feat_grad, weight_grad)


def solution(mesh):
    in_specs = (
        P(("row", "col"), None),
        P(),
        P(("row", "col"), None),
        P(("row", "col"), None, None),
        P(("row", "col"), None),
        P(("row", "col"), None, None),
        P(("row", "col"), None),
        P(("row", "col")),
        P(("row", "col"), None),
        P(("row", "col"), None),
        P(("row", "col"), None),
    )
    out_specs = (P(("row", "col"), None), P(("row", "col"), None), P())
    return jax.shard_map(
        on_device, mesh=mesh, in_specs=in_specs, out_specs=out_specs, check_vma=False
    )
```

profile of v0, /device:TPU:0, one launch (start us, length us, event | category | flops | bytes accessed | tf_op | source)
XLA Modules:
  0.0 214.7 jit_solution(14946147041477789685)
XLA Ops:
  7.2 0.0 copy-start
  7.2 0.0 copy-start.11
  7.2 0.0 copy-start.9
  7.2 0.0 copy-start.3
  7.2 0.8 compare_select_fusion.2
  8.0 0.7 compare_and_fusion.1
  8.7 1.9 gather_fusion.3
  10.6 0.0 copy-start.6
  10.6 0.2 convolution_convert_fusion.1
  10.9 0.5 collective-permute-start
  11.4 2.0 collective-permute-start.1
  13.4 0.7 maximum_bitcast_fusion
  14.0 0.7 broadcast_compare_fusion
  14.7 0.6 gather_fusion
  15.3 0.0 copy-start.2
  15.3 0.9 select_select_fusion
  16.3 6.5 %all-to-all-start = ((bf16[8,128,256]{2,1,0:T(8,128)(2,1)}), bf16[8,128,256]{2,1,0:T(8,128)(2,1)S(1)}, u32[]{:S(2)}, u32[]{:S(2)}) async-start(bf16[8,128,256]{2,1,0:T(8,128)(2,1)} %select_select_fusion), calls=%async_computation | async-start | bytes 1048576 | tf_op jit(solution)/shard_map/all_to_all | solution.py:77
  22.8 0.6 compare_select_fusion
  23.4 0.6 slice_bitcast_fusion
  24.6 0.6 iota_compare_fusion.1
  25.2 0.8 copy.20
  26.1 0.0 copy-start.10
  26.1 1.8 gather_fusion.5
  27.9 0.1 broadcast_in_dim.61
  28.0 2.0 scatter_fusion
  30.1 1.1 copy.19
  31.2 2.1 scatter_custom_fusion.1
  33.3 0.5 and_bitcast_fusion
  33.8 1.7 broadcast_multiply_fusion
  35.6 1.8 all-to-all-done
  37.3 0.7 gather_fusion.1
  38.1 0.3 broadcast_select_fusion
  38.4 1.4 copy-done.4
  39.8 0.8 fusion.1
  40.7 0.0 collective-permute-done
  40.7 0.1 copy-done.5
  40.8 0.0 copy-done.8
  40.8 1.3 multiply_convert_fusion
  42.2 0.0 copy-start.16
  42.2 2.4 %gather_fusion.2 = bf16[40,128,256]{2,1,0:T(8,128)(2,1)} fusion(bf16[2,128,256]{2,1,0:T(8,128)(2,1)S(1)} %bitcast.73, s32[1024]{0:T(1024)S(1)} %pad_clamp_fusion), kind=kCustom, calls=%fused_computation.6 | custom fusion | bytes 5243040 | tf_op jit(solution)/shard_map/jit(_take)/gather | solution.py:111
  44.6 4.9 %fusion = (bf16[40,128,256]{1,2,0:T(8,128)(2,1)S(1)}, bf16[40,128,256]{1,2,0:T(8,128)(2,1)}) fusion(bf16[40,128,128]{2,1,0:T(8,128)(2,1)} %param.26, bf16[40,128,256]{2,1,0:T(8,128)(2,1)} %gather_fusion.2, pred[40]{0:T(512)(128)(4,1)S(1)} %copy-done.16), kind=kOutput, calls=%fused_computation.11 | convolution fusion | flops 342097920 | bytes 9175080 | tf_op jit(solution)/shard_map/kab,kaf->kbf/dot_general | solution.py:108
  49.5 4.7 %copy.22 = bf16[40,128,256]{2,0,1:T(8,128)(2,1)} copy(bf16[40,128,256]{1,2,0:T(8,128)(2,1)} %get-tuple-element.45) | data formatting | bytes 5242880 | tf_op jit(solution)/shard_map/convert_element_type | solution.py:26
  54.2 3.4 %copy.23 = bf16[40,128,256]{2,0,1:T(8,128)(2,1)} copy(bf16[40,128,256]{1,2,0:T(8,128)(2,1)S(1)} %get-tuple-element.44) | data formatting | bytes 5242880 | tf_op jit(solution)/shard_map/convert_element_type | solution.py:27
  57.6 2.5 %fusion.28 = f32[8,128,256]{2,0,1:T(8,128)S(1)} fusion(bf16[40,128,256]{2,0,1:T(8,128)(2,1)} %copy.22, s32[40]{0:T(128)S(1)} %get-tuple-element.50, pred[40]{0:T(512)(128)(4,1)S(1)} %copy-done.15), kind=kOutput, calls=%fused_computation.62 | convolution fusion | flops 20972160 | bytes 3670216 | tf_op jit(solution)/shard_map/rk,kaf->raf/dot_general | solution.py:29
  60.0 0.1 copy-done.1
  60.1 0.6 fusion.8
  60.7 0.9 copy.24
  61.6 4.2 %all-to-all-start.1 = ((bf16[8,128,256]{2,1,0:T(8,128)(2,1)}), bf16[8,128,256]{2,1,0:T(8,128)(2,1)S(1)}, u32[]{:S(2)}, u32[]{:S(2)}) async-start(bf16[8,128,256]{2,1,0:T(8,128)(2,1)} %copy.24), calls=%async_computation.1 | async-start | bytes 1048576 | tf_op jit(solution)/shard_map/all_to_all | solution.py:117
  65.8 0.0 all-reduce.2.cloned.1.call-start
  65.9 0.0 copy-start.7
  65.9 0.3 fusion.50
  66.2 0.1 collective-permute-start.2
  66.3 1.7 collective-permute-start.3
  68.0 1.1 gather_fusion.4
  69.2 10.8 %all-to-all-done.1 = bf16[8,128,256]{2,1,0:T(8,128)(2,1)S(1)} async-done(((bf16[8,128,256]{2,1,0:T(8,128)(2,1)}), bf16[8,128,256]{2,1,0:T(8,128)(2,1)S(1)}, u32[]{:S(2)}, u32[]{:S(2)}) %all-to-all-start.1) | async-done | bytes 524320 | tf_op jit(solution)/shard_map/all_to_all | solution.py:117
  79.9 0.4 fusion.9
  80.4 0.1 fusion.23
  80.4 0.2 convolution_convert_fusion
  80.7 1.0 fusion.24
  81.7 1.1 gather_fusion.6
  82.8 0.0 all-reduce.2.cloned.1.call-update
  82.9 0.8 broadcast_select_fusion.1
  83.7 122.5 %all-reduce.2.cloned.1.call-done = f32[256,256]{1,0:T(8,128)} async-done(((f32[256,256]{1,0:T(8,128)}), f32[256,256]{1,0:T(8,128)}) %all-reduce.2.cloned.1.call-update) | async-done | bytes 262160 | tf_op jit(solution)/shard_map/psum | solution.py:128
  206.1 1.7 broadcast_multiply_fusion.1
  (46 shorter events, 0.2 us)
Async XLA Ops:
  7.2 3.4 %copy-start = (bf16[256,256]{1,0:T(8,128)(2,1)S(1)}, bf16[256,256]{1,0:T(8,128)(2,1)}, u32[]{:S(2)}) copy-start(bf16[256,256]{1,0:T(8,128)(2,1)} %param.22) | copy-start | bytes 393220
  7.2 15.6 %copy-start.11 = (s32[1,256]{1,0:T(1,128)S(1)}, s32[1,256]{1,0:T(1,128)}, u32[]{:S(2)}) copy-start(s32[1,256]{1,0:T(1,128)} %param.30) | copy-start | bytes 3076
  7.2 16.2 %copy-start.9 = (s32[40,2]{0,1:T(2,128)S(1)}, s32[40,2]{0,1:T(2,128)}, u32[]{:S(2)}) copy-start(s32[40,2]{0,1:T(2,128)} %param.27) | copy-start | bytes 964
  7.2 17.4 %copy-start.21 = (s32[12,2]{0,1:T(2,128)S(1)}, s32[12,2]{0,1:T(2,128)}, u32[]{:S(2)}) copy-start(s32[12,2]{0,1:T(2,128)} %param.25) | copy-start | bytes 292
  7.2 18.0 %copy-start.3 = (bf16[40,128,128]{2,1,0:T(8,128)(2,1)S(1)}, bf16[40,128,128]{2,1,0:T(8,128)(2,1)}, u32[]{:S(2)}) copy-start(bf16[40,128,128]{2,1,0:T(8,128)(2,1)} %param.26) | copy-start | bytes 3932164
  8.7 5.3 %copy-start.12 = (pred[256]{0:T(512)(128)(4,1)}, pred[256]{0:T(512)(128)(4,1)S(1)}, u32[]{:S(2)}) copy-start(pred[256]{0:T(512)(128)(4,1)S(1)} %compare_and_fusion.1) | copy-start | bytes 772
  10.6 4.1 %copy-start.6 = (bf16[256,256]{1,0:T(8,128)(2,1)}, bf16[256,256]{1,0:T(8,128)(2,1)S(1)}, u32[]{:S(2)}) copy-start(bf16[256,256]{1,0:T(8,128)(2,1)S(1)} %gather_fusion.3) | copy-start | bytes 393220
  10.9 29.8 %collective-permute-start = (bf16[256,256]{1,0:T(8,128)(2,1)S(1)}, bf16[256,256]{1,0:T(8,128)(2,1)}, u32[]{:S(2)}, u32[]{:S(2)}) collective-permute-start(bf16[256,256]{1,0:T(8,128)(2,1)S(1)} %convolution_convert_fusion.1), channel_id=1, source_target_pairs={{0,8},{8,16},{16,24},{24,0},{1,9},{9,17},{17,25},{25,1},{2,10},{10... | collective-permute-start | bytes 393224 | tf_op jit(solution)/shard_map/ppermute | solution.py:16
  11.4 29.3 %collective-permute-start.1 = (bf16[256,256]{1,0:T(8,128)(2,1)S(1)}, bf16[256,256]{1,0:T(8,128)(2,1)}, u32[]{:S(2)}, u32[]{:S(2)}) collective-permute-start(bf16[256,256]{1,0:T(8,128)(2,1)S(1)} %convolution_convert_fusion.1), channel_id=1, source_target_pairs={{8,0},{16,8},{24,16},{0,24},{9,1},{17,9},{25,17},{1,25},{10,2},{18... | collective-permute-start | bytes 393224 | tf_op jit(solution)/shard_map/ppermute | solution.py:18
  15.3 10.8 %copy-start.2 = (bf16[256,256]{1,0:T(8,128)(2,1)S(1)}, bf16[256,256]{1,0:T(8,128)(2,1)}, u32[]{:S(2)}) copy-start(bf16[256,256]{1,0:T(8,128)(2,1)} %param.23) | copy-start | bytes 393220
  16.3 21.1 %all-to-all-start = ((bf16[8,128,256]{2,1,0:T(8,128)(2,1)}), bf16[8,128,256]{2,1,0:T(8,128)(2,1)S(1)}, u32[]{:S(2)}, u32[]{:S(2)}) async-start(bf16[8,128,256]{2,1,0:T(8,128)(2,1)} %select_select_fusion), calls=%async_computation | async-start | bytes 1048576 | tf_op jit(solution)/shard_map/all_to_all | solution.py:77
  26.1 7.2 %copy-start.17 = (s32[40]{0:T(128)S(1)}, s32[40]{0:T(128)}, u32[]{:S(2)}) copy-start(s32[40]{0:T(128)} %get-tuple-element.51) | copy-start | bytes 484
  26.1 7.2 %copy-start.14 = (pred[40]{0:T(512)(128)(4,1)S(1)}, pred[40]{0:T(512)(128)(4,1)}, u32[]{:S(2)}) copy-start(pred[40]{0:T(512)(128)(4,1)} %iota_compare_fusion.1) | copy-start | bytes 124
  26.1 7.2 %copy-start.19 = (s32[40]{0:T(128)S(1)}, s32[40]{0:T(128)}, u32[]{:S(2)}) copy-start(s32[40]{0:T(128)} %get-tuple-element.53) | copy-start | bytes 484
  26.1 7.2 %copy-start.10 = (s32[40,2]{0,1:T(2,128)S(1)}, s32[40,2]{0,1:T(2,128)}, u32[]{:S(2)}) copy-start(s32[40,2]{0,1:T(2,128)} %param.27) | copy-start | bytes 964
  38.1 1.7 copy-start.4
  39.8 1.0 copy-start.5
  39.8 1.0 copy-start.8
  39.8 1.0 copy-start.13
  42.2 2.4 %copy-start.16 = (pred[40]{0:T(512)(128)(4,1)S(1)}, pred[40]{0:T(512)(128)(4,1)}, u32[]{:S(2)}) copy-start(pred[40]{0:T(512)(128)(4,1)} %get-tuple-element.54) | copy-start | bytes 124
  54.2 3.4 %copy-start.15 = (pred[40]{0:T(512)(128)(4,1)S(1)}, pred[40]{0:T(512)(128)(4,1)}, u32[]{:S(2)}) copy-start(pred[40]{0:T(512)(128)(4,1)} %iota_compare_fusion.1) | copy-start | bytes 124
  57.6 2.5 %copy-start.1 = (bf16[40,128,256]{2,0,1:T(8,128)(2,1)S(1)}, bf16[40,128,256]{2,0,1:T(8,128)(2,1)}, u32[]{:S(2)}) copy-start(bf16[40,128,256]{2,0,1:T(8,128)(2,1)} %copy.23) | copy-start | bytes 7864324
  60.1 5.8 %copy-start.18 = (s32[256]{0:T(256)S(1)}, s32[256]{0:T(256)}, u32[]{:S(2)}) copy-start(s32[256]{0:T(256)} %scatter_custom_fusion.1) | copy-start | bytes 3076
  60.7 19.3 %copy-start.20 = (s32[1,8]{1,0:T(1,128)S(1)}, s32[1,8]{1,0:T(1,128)}, u32[]{:S(2)}) copy-start(s32[1,8]{1,0:T(1,128)} %param.29) | copy-start | bytes 100
  61.6 18.4 %all-to-all-start.1 = ((bf16[8,128,256]{2,1,0:T(8,128)(2,1)}), bf16[8,128,256]{2,1,0:T(8,128)(2,1)S(1)}, u32[]{:S(2)}, u32[]{:S(2)}) async-start(bf16[8,128,256]{2,1,0:T(8,128)(2,1)} %copy.24), calls=%async_computation.1 | async-start | bytes 1048576 | tf_op jit(solution)/shard_map/all_to_all | solution.py:117
  65.8 140.3 %all-reduce.2.cloned.1.call-start = ((), (), s32[]{:S(2)}) async-start(), calls=%async_computation.2 | async-start | bytes 524288 | tf_op jit(solution)/shard_map/psum | solution.py:128
  65.9 14.8 %copy-start.7 = (bf16[256,256]{1,0:T(8,128)(2,1)S(1)}, bf16[256,256]{1,0:T(8,128)(2,1)}, u32[]{:S(2)}) copy-start(bf16[256,256]{1,0:T(8,128)(2,1)} %copy-done.6) | copy-start | bytes 393220
  66.2 14.1 %collective-permute-start.2 = (bf16[256,256]{1,0:T(8,128)(2,1)S(1)}, bf16[256,256]{1,0:T(8,128)(2,1)S(1)}, u32[]{:S(2)}, u32[]{:S(2)}) collective-permute-start(bf16[256,256]{1,0:T(8,128)(2,1)S(1)} %get-tuple-element.46), channel_id=1, source_target_pairs={{0,8},{8,16},{16,24},{24,0},{1,9},{9,17},{17,25},{25,1},{2,10},{10... | collective-permute-start | bytes 393224 | tf_op jit(solution)/shard_map/ppermute | solution.py:16
  66.3 14.1 %collective-permute-start.3 = (bf16[256,256]{1,0:T(8,128)(2,1)S(1)}, bf16[256,256]{1,0:T(8,128)(2,1)S(1)}, u32[]{:S(2)}, u32[]{:S(2)}) collective-permute-start(bf16[256,256]{1,0:T(8,128)(2,1)S(1)} %get-tuple-element.47), channel_id=1, source_target_pairs={{8,0},{16,8},{24,16},{0,24},{9,1},{17,9},{25,17},{1,25},{10,2},{18... | collective-permute-start | bytes 393224 | tf_op jit(solution)/shard_map/ppermute | solution.py:18
Sparse Core Ops, SparseCore 0:
  83.0 123.1 all-reduce.1
where the time goes:
time: 215 us
  waiting for transfers between devices  135 us (63%)
  local copies, waits for them, and re-layouts  26.5 us (12%)
  starting transfers between devices  15.1 us (7%)
  between operations  15.1 us (7%)
  matrix products  12.3 us (6%)
  other arithmetic  10.6 us (5%)
    psum x1, waiting for transfers between devices, on_device(): weight_grad = lax.psum(partial_weight, ('row', 'col')) * nodes_all ** (-0.5)  122 us
    all_to_all x1, waiting for transfers between devices, on_device(): lax.all_to_all(to_owner, 'col', split_axis=0, concat_axis=0, tiled=True)  10.8 us
    all_to_all x1, starting transfers between devices, on_device(): lax.all_to_all(outgoing, 'col', split_axis=0, concat_axis=0, tiled=True)  6.53 us
    dot_general x1, matrix products, on_device(): jnp.einsum('kab,kaf->kbf', bound_tiles, jnp.take(slope_blocks, bound_row_...  4.94 us
    convert_element_type x1, local copies, waits for them, and re-layouts, split_sum(): high_part = terms.astype(jnp.bfloat16)  4.69 us
  transfers between devices with their start and end apart: 7, of which 3 were waited for; matrix products, arithmetic and copies ran while one was open for 9% of the time, Pallas kernels for 0%

commit v1 on v0

--- a/solution.py
+++ b/solution.py
@@ -74,7 +74,18 @@
         jnp.take(blocks, jnp.maximum(giving, 0), axis=0),
         jnp.zeros((), jnp.bfloat16),
     )
-    arrived = lax.all_to_all(outgoing, "col", split_axis=0, concat_axis=0, tiled=True)
+    ways, here = (lax.axis_size("col"), lax.axis_index("col"))
+    width_2 = outgoing.shape[0] // ways
+    shape = list(outgoing.shape)
+    shape[0] = width_2
+    height = shape[0]
+    shape[0] = height * ways
+    arrived = jnp.zeros(shape, outgoing.dtype)
+    for mask in range(ways):
+        part = lax.dynamic_slice_in_dim(outgoing, (here ^ mask) * width_2, width_2, axis=0)
+        if mask:
+            part = lax.ppermute(part, "col", [(d, d ^ mask) for d in range(ways)])
+        arrived = lax.dynamic_update_slice_in_dim(arrived, part, (here ^ mask) * height, axis=0)
     tile_range = jnp.arange(tile_rows, dtype=jnp.int32)
     live_slots = jnp.arange(slot_total, dtype=jnp.int32) < bound_count[0]
     bound_row_ids = bound_coords[:, 0]

time: 215 us -> 227 us (1.056)
  starting transfers between devices: 15.1 us -> 20.1 us
  local copies, waits for them, and re-layouts: 26.5 us -> 29.9 us
  waiting for transfers between devices: 135 us -> 138 us
    ppermute x0 -> x7, starting transfers between devices: none -> 13.5 us  [on_device(): part = lax.ppermute(part, 'col', [(d, d ^ mask) for d in range(ways)])]
    all_to_all x1 -> x0, starting transfers between devices: 6.53 us -> none  [on_device(): lax.all_to_all(outgoing, 'col', split_axis=0, concat_axis=0, tiled=True)]
    ppermute x0 -> x7, waiting for transfers between devices: none -> 5.38 us  [on_device(): part = lax.ppermute(part, 'col', [(d, d ^ mask) for d in range(ways)])]
    dynamic_update_slice x0 -> x7, local copies, waits for them, and re-layouts: none -> 2.57 us  [on_device(): lax.dynamic_update_slice_in_dim(arrived, part, (here ^ mask) * height, ax...]
  transfers between devices with their start and end apart: 7 -> 13, of which waited for: 3 -> 4; matrix products, arithmetic and copies ran while one was open for 9% -> 10% of each run, Pallas kernels for 0% -> 0%
where the time goes in v1:
time: 227 us; the launch traced here: 226 us
  waiting for transfers between devices  138 us (61%)
  local copies, waits for them, and re-layouts  29.9 us (13%)
  starting transfers between devices  20.1 us (9%)
  between operations  15.2 us (7%)
  matrix products  12.3 us (5%)
  other arithmetic  10.5 us (5%)
    psum x1, waiting for transfers between devices, on_device(): weight_grad = lax.psum(partial_weight, ('row', 'col')) * nodes_all ** (-0.5)  123 us
    ppermute x7, starting transfers between devices, on_device(): part = lax.ppermute(part, 'col', [(d, d ^ mask) for d in range(ways)])  13.5 us
    all_to_all x1, waiting for transfers between devices, on_device(): lax.all_to_all(to_owner, 'col', split_axis=0, concat_axis=0, tiled=True)  10 us
    ppermute x7, waiting for transfers between devices, on_device(): part = lax.ppermute(part, 'col', [(d, d ^ mask) for d in range(ways)])  5.38 us
    dot_general x1, matrix products, on_device(): jnp.einsum('kab,kaf->kbf', bound_tiles, jnp.take(slope_blocks, bound_row_...  4.93 us
    convert_element_type x1, local copies, waits for them, and re-layouts, split_sum(): high_part = terms.astype(jnp.bfloat16)  4.74 us
  transfers between devices with their start and end apart: 13, of which 4 were waited for; matrix products, arithmetic and copies ran while one was open for 10% of the time, Pallas kernels for 0%

profile of v1, /device:TPU:0, one launch (start us, length us, event | category | flops | bytes accessed | tf_op | source)
XLA Modules:
  0.0 226.0 jit_solution(1143045340061211109)
XLA Ops:
  7.2 0.7 compare_select_fusion.2
  7.9 0.7 compare_and_fusion.1
  8.6 2.0 gather_fusion.3
  10.6 0.2 convolution_convert_fusion.1
  10.9 0.5 collective-permute-start
  11.4 2.0 collective-permute-start.1
  13.4 0.7 maximum_bitcast_fusion
  14.1 0.7 broadcast_compare_fusion
  14.8 0.6 gather_fusion
  15.4 0.1 select_select_fusion
  15.6 0.8 constant_dynamic-slice_fusion
  16.4 2.2 collective-permute-start.2
  18.6 1.6 collective-permute-start.3
  20.1 0.6 slice_bitcast_fusion
  20.7 0.6 and_bitcast_fusion
  21.3 0.6 compare_select_fusion
  22.6 0.5 iota_compare_fusion.1
  23.1 0.8 copy.20
  24.0 1.8 gather_fusion.5
  25.8 0.8 fusion.42
  26.6 0.1 broadcast_in_dim.62
  26.6 2.0 scatter_fusion
  28.7 1.1 copy.19
  29.8 1.7 broadcast_multiply_fusion
  31.6 2.0 scatter_custom_fusion.1
  33.6 3.1 %collective-permute-start.5 = (bf16[1,128,256]{2,1,0:T(8,128)(2,1)S(1)}, bf16[1,128,256]{2,1,0:T(8,128)(2,1)S(1)}, u32[]{:S(2)}, u32[]{:S(2)}) collective-permute-start(bf16[1,128,256]{2,1,0:T(8,128)(2,1)S(1)} %copy-done.12), channel_id=1, source_target_pairs={{0,4},{1,5},{2,6},{3,7},{4,0},{5,1},{6,2},{7,3},{8,12},{9,13},{10,... | collective-permute-start | bytes 196616 | tf_op jit(solution)/shard_map/ppermute | solution.py:87
  36.7 0.8 constant_dynamic-update-slice_fusion.6
  37.6 1.3 collective-permute-start.6
  38.9 0.8 constant_dynamic-update-slice_fusion.5
  39.7 3.7 %collective-permute-start.7 = (bf16[1,128,256]{2,1,0:T(8,128)(2,1)S(1)}, bf16[1,128,256]{2,1,0:T(8,128)(2,1)S(1)}, u32[]{:S(2)}, u32[]{:S(2)}) collective-permute-start(bf16[1,128,256]{2,1,0:T(8,128)(2,1)S(1)} %copy-done.10), channel_id=1, source_target_pairs={{0,6},{1,7},{2,4},{3,5},{4,2},{5,3},{6,0},{7,1},{8,14},{9,15},{10,... | collective-permute-start | bytes 196616 | tf_op jit(solution)/shard_map/ppermute | solution.py:87
  43.4 0.8 constant_dynamic-update-slice_fusion.4
  44.3 1.6 collective-permute-start.8
  45.9 0.4 collective-permute-done.6
  46.4 4.9 %collective-permute-done.8 = bf16[1,128,256]{2,1,0:T(8,128)(2,1)S(1)} collective-permute-done((bf16[1,128,256]{2,1,0:T(8,128)(2,1)S(1)}, bf16[1,128,256]{2,1,0:T(8,128)(2,1)S(1)}, u32[]{:S(2)}, u32[]{:S(2)}) %collective-permute-start.8) | collective-permute-done | bytes 65568 | tf_op jit(solution)/shard_map/ppermute | solution.py:87
  51.3 0.7 gather_fusion.1
  52.1 0.3 broadcast_select_fusion
  52.4 1.4 copy-done.4
  53.8 0.8 fusion.1
  54.7 0.1 copy-done.5
  54.8 0.0 copy-done.8
  54.8 1.3 multiply_convert_fusion
  56.2 2.4 %gather_fusion.2 = bf16[40,128,256]{2,1,0:T(8,128)(2,1)} fusion(bf16[2,128,256]{2,1,0:T(8,128)(2,1)S(1)} %bitcast.73, s32[1024]{0:T(1024)S(1)} %pad_clamp_fusion), kind=kCustom, calls=%fused_computation.6 | custom fusion | bytes 5243040 | tf_op jit(solution)/shard_map/jit(_take)/gather | solution.py:122
  58.5 4.9 %fusion = (bf16[40,128,256]{1,2,0:T(8,128)(2,1)S(1)}, bf16[40,128,256]{1,2,0:T(8,128)(2,1)}) fusion(bf16[40,128,128]{2,1,0:T(8,128)(2,1)} %param.26, bf16[40,128,256]{2,1,0:T(8,128)(2,1)} %gather_fusion.2, pred[40]{0:T(512)(128)(4,1)S(1)} %copy-done.17), kind=kOutput, calls=%fused_computation.11 | convolution fusion | flops 342097920 | bytes 9175080 | tf_op jit(solution)/shard_map/kab,kaf->kbf/dot_general | solution.py:119
  63.4 4.7 %copy.22 = bf16[40,128,256]{2,0,1:T(8,128)(2,1)} copy(bf16[40,128,256]{1,2,0:T(8,128)(2,1)} %get-tuple-element.45) | data formatting | bytes 5242880 | tf_op jit(solution)/shard_map/convert_element_type | solution.py:26
  68.2 3.4 %copy.23 = bf16[40,128,256]{2,0,1:T(8,128)(2,1)} copy(bf16[40,128,256]{1,2,0:T(8,128)(2,1)S(1)} %get-tuple-element.44) | data formatting | bytes 5242880 | tf_op jit(solution)/shard_map/convert_element_type | solution.py:27
  71.6 2.5 %fusion.28 = f32[8,128,256]{2,0,1:T(8,128)S(1)} fusion(bf16[40,128,256]{2,0,1:T(8,128)(2,1)} %copy.22, s32[40]{0:T(128)S(1)} %get-tuple-element.58, pred[40]{0:T(512)(128)(4,1)S(1)} %copy-done.16), kind=kOutput, calls=%fused_computation.77 | convolution fusion | flops 20972160 | bytes 3670216 | tf_op jit(solution)/shard_map/rk,kaf->raf/dot_general | solution.py:29
  74.0 0.1 copy-done.1
  74.1 0.6 fusion.8
  74.7 0.9 copy.24
  75.5 3.5 %all-to-all-start = ((bf16[8,128,256]{2,1,0:T(8,128)(2,1)}), bf16[8,128,256]{2,1,0:T(8,128)(2,1)S(1)}, u32[]{:S(2)}, u32[]{:S(2)}) async-start(bf16[8,128,256]{2,1,0:T(8,128)(2,1)} %copy.24), calls=%async_computation | async-start | bytes 1048576 | tf_op jit(solution)/shard_map/all_to_all | solution.py:128
  79.0 0.0 all-reduce.2.cloned.1.call-start
  79.2 0.3 fusion.50
  79.5 0.1 collective-permute-start.10
  79.5 0.5 collective-permute-start.9
  80.0 1.1 gather_fusion.4
  81.2 10.0 %all-to-all-done = bf16[8,128,256]{2,1,0:T(8,128)(2,1)S(1)} async-done(((bf16[8,128,256]{2,1,0:T(8,128)(2,1)}), bf16[8,128,256]{2,1,0:T(8,128)(2,1)S(1)}, u32[]{:S(2)}, u32[]{:S(2)}) %all-to-all-start) | async-done | bytes 524320 | tf_op jit(solution)/shard_map/all_to_all | solution.py:128
  91.2 0.4 fusion.9
  91.6 0.1 fusion.23
  91.7 0.2 convolution_convert_fusion
  91.9 1.0 fusion.24
  93.0 1.1 gather_fusion.6
  94.1 0.8 broadcast_select_fusion.1
  94.9 122.5 %all-reduce.2.cloned.1.call-done = f32[256,256]{1,0:T(8,128)} async-done(((f32[256,256]{1,0:T(8,128)}), f32[256,256]{1,0:T(8,128)}) %all-reduce.2.cloned.1.call-update) | async-done | bytes 262160 | tf_op jit(solution)/shard_map/psum | solution.py:139
  217.4 1.7 broadcast_multiply_fusion.1
  (69 shorter events, 0.3 us)
Async XLA Ops:
  7.2 3.5 %copy-start = (bf16[256,256]{1,0:T(8,128)(2,1)S(1)}, bf16[256,256]{1,0:T(8,128)(2,1)}, u32[]{:S(2)}) copy-start(bf16[256,256]{1,0:T(8,128)(2,1)} %param.22) | copy-start | bytes 393220
  8.6 11.6 %copy-start.13 = (s32[40,2]{0,1:T(2,128)S(1)}, s32[40,2]{0,1:T(2,128)}, u32[]{:S(2)}) copy-start(s32[40,2]{0,1:T(2,128)} %param.27) | copy-start | bytes 964
  8.6 12.7 %copy-start.14 = (s32[1,256]{1,0:T(1,128)S(1)}, s32[1,256]{1,0:T(1,128)}, u32[]{:S(2)}) copy-start(s32[1,256]{1,0:T(1,128)} %param.30) | copy-start | bytes 3076
  8.6 14.5 %copy-start.3 = (bf16[40,128,128]{2,1,0:T(8,128)(2,1)S(1)}, bf16[40,128,128]{2,1,0:T(8,128)(2,1)}, u32[]{:S(2)}) copy-start(bf16[40,128,128]{2,1,0:T(8,128)(2,1)} %param.26) | copy-start | bytes 3932164
  10.6 4.1 %copy-start.6 = (bf16[256,256]{1,0:T(8,128)(2,1)}, bf16[256,256]{1,0:T(8,128)(2,1)S(1)}, u32[]{:S(2)}) copy-start(bf16[256,256]{1,0:T(8,128)(2,1)S(1)} %gather_fusion.3) | copy-start | bytes 393220
  10.9 43.8 %collective-permute-start = (bf16[256,256]{1,0:T(8,128)(2,1)S(1)}, bf16[256,256]{1,0:T(8,128)(2,1)}, u32[]{:S(2)}, u32[]{:S(2)}) collective-permute-start(bf16[256,256]{1,0:T(8,128)(2,1)S(1)} %convolution_convert_fusion.1), channel_id=1, source_target_pairs={{0,8},{8,16},{16,24},{24,0},{1,9},{9,17},{17,25},{25,1},{2,10},{10... | collective-permute-start | bytes 393224 | tf_op jit(solution)/shard_map/ppermute | solution.py:16
  11.4 43.3 %collective-permute-start.1 = (bf16[256,256]{1,0:T(8,128)(2,1)S(1)}, bf16[256,256]{1,0:T(8,128)(2,1)}, u32[]{:S(2)}, u32[]{:S(2)}) collective-permute-start(bf16[256,256]{1,0:T(8,128)(2,1)S(1)} %convolution_convert_fusion.1), channel_id=1, source_target_pairs={{8,0},{16,8},{24,16},{0,24},{9,1},{17,9},{25,17},{1,25},{10,2},{18... | collective-permute-start | bytes 393224 | tf_op jit(solution)/shard_map/ppermute | solution.py:18
  15.4 8.6 %copy-start.2 = (bf16[256,256]{1,0:T(8,128)(2,1)S(1)}, bf16[256,256]{1,0:T(8,128)(2,1)}, u32[]{:S(2)}) copy-start(bf16[256,256]{1,0:T(8,128)(2,1)} %param.23) | copy-start | bytes 393220
  16.4 17.3 %collective-permute-start.2 = (bf16[1,128,256]{2,1,0:T(8,128)(2,1)}, bf16[1,128,256]{2,1,0:T(8,128)(2,1)}, u32[]{:S(2)}, u32[]{:S(2)}) collective-permute-start(bf16[1,128,256]{2,1,0:T(8,128)(2,1)} %get-tuple-element.52), channel_id=1, source_target_pairs={{0,1},{1,0},{2,3},{3,2},{4,5},{5,4},{6,7},{7,6},{8,9},{9,8},{10,11... | collective-permute-start | bytes 196616 | tf_op jit(solution)/shard_map/ppermute | solution.py:87
  18.6 19.0 %collective-permute-start.3 = (bf16[1,128,256]{2,1,0:T(8,128)(2,1)}, bf16[1,128,256]{2,1,0:T(8,128)(2,1)}, u32[]{:S(2)}, u32[]{:S(2)}) collective-permute-start(bf16[1,128,256]{2,1,0:T(8,128)(2,1)} %get-tuple-element.51), channel_id=1, source_target_pairs={{0,2},{1,3},{2,0},{3,1},{4,6},{5,7},{6,4},{7,5},{8,10},{9,11},{10,... | collective-permute-start | bytes 196616 | tf_op jit(solution)/shard_map/ppermute | solution.py:87
  20.1 19.6 %collective-permute-start.4 = (bf16[1,128,256]{2,1,0:T(8,128)(2,1)}, bf16[1,128,256]{2,1,0:T(8,128)(2,1)}, u32[]{:S(2)}, u32[]{:S(2)}) collective-permute-start(bf16[1,128,256]{2,1,0:T(8,128)(2,1)} %get-tuple-element.50), channel_id=1, source_target_pairs={{0,3},{1,2},{2,1},{3,0},{4,7},{5,6},{6,5},{7,4},{8,11},{9,10},{10,... | collective-permute-start | bytes 196616 | tf_op jit(solution)/shard_map/ppermute | solution.py:87
  24.0 5.8 %copy-start.15 = (pred[40]{0:T(512)(128)(4,1)S(1)}, pred[40]{0:T(512)(128)(4,1)}, u32[]{:S(2)}) copy-start(pred[40]{0:T(512)(128)(4,1)} %iota_compare_fusion.1) | copy-start | bytes 124
  24.0 5.8 %copy-start.21 = (s32[40]{0:T(128)S(1)}, s32[40]{0:T(128)}, u32[]{:S(2)}) copy-start(s32[40]{0:T(128)} %get-tuple-element.61) | copy-start | bytes 484
  28.7 4.9 %copy-start.18 = (s32[40]{0:T(128)S(1)}, s32[40]{0:T(128)}, u32[]{:S(2)}) copy-start(s32[40]{0:T(128)} %get-tuple-element.59) | copy-start | bytes 484
  28.7 4.9 %copy-start.12 = (bf16[1,128,256]{2,1,0:T(8,128)(2,1)S(1)}, bf16[1,128,256]{2,1,0:T(8,128)(2,1)}, u32[]{:S(2)}) copy-start(bf16[1,128,256]{2,1,0:T(8,128)(2,1)} %get-tuple-element.49) | copy-start | bytes 196612
  28.7 8.8 %copy-start.11 = (bf16[1,128,256]{2,1,0:T(8,128)(2,1)S(1)}, bf16[1,128,256]{2,1,0:T(8,128)(2,1)}, u32[]{:S(2)}) copy-start(bf16[1,128,256]{2,1,0:T(8,128)(2,1)} %get-tuple-element.48) | copy-start | bytes 196612
  28.7 11.0 %copy-start.10 = (bf16[1,128,256]{2,1,0:T(8,128)(2,1)S(1)}, bf16[1,128,256]{2,1,0:T(8,128)(2,1)}, u32[]{:S(2)}) copy-start(bf16[1,128,256]{2,1,0:T(8,128)(2,1)} %get-tuple-element.47) | copy-start | bytes 196612
  28.7 15.5 %copy-start.9 = (bf16[1,128,256]{2,1,0:T(8,128)(2,1)S(1)}, bf16[1,128,256]{2,1,0:T(8,128)(2,1)}, u32[]{:S(2)}) copy-start(bf16[1,128,256]{2,1,0:T(8,128)(2,1)} %get-tuple-element.46) | copy-start | bytes 196612
  33.6 10.6 %collective-permute-start.5 = (bf16[1,128,256]{2,1,0:T(8,128)(2,1)S(1)}, bf16[1,128,256]{2,1,0:T(8,128)(2,1)S(1)}, u32[]{:S(2)}, u32[]{:S(2)}) collective-permute-start(bf16[1,128,256]{2,1,0:T(8,128)(2,1)S(1)} %copy-done.12), channel_id=1, source_target_pairs={{0,4},{1,5},{2,6},{3,7},{4,0},{5,1},{6,2},{7,3},{8,12},{9,13},{10,... | collective-permute-start | bytes 196616 | tf_op jit(solution)/shard_map/ppermute | solution.py:87
  37.6 8.8 %collective-permute-start.6 = (bf16[1,128,256]{2,1,0:T(8,128)(2,1)S(1)}, bf16[1,128,256]{2,1,0:T(8,128)(2,1)S(1)}, u32[]{:S(2)}, u32[]{:S(2)}) collective-permute-start(bf16[1,128,256]{2,1,0:T(8,128)(2,1)S(1)} %copy-done.11), channel_id=1, source_target_pairs={{0,5},{1,4},{2,7},{3,6},{4,1},{5,0},{6,3},{7,2},{8,13},{9,12},{10,... | collective-permute-start | bytes 196616 | tf_op jit(solution)/shard_map/ppermute | solution.py:87
  39.7 6.6 %collective-permute-start.7 = (bf16[1,128,256]{2,1,0:T(8,128)(2,1)S(1)}, bf16[1,128,256]{2,1,0:T(8,128)(2,1)S(1)}, u32[]{:S(2)}, u32[]{:S(2)}) collective-permute-start(bf16[1,128,256]{2,1,0:T(8,128)(2,1)S(1)} %copy-done.10), channel_id=1, source_target_pairs={{0,6},{1,7},{2,4},{3,5},{4,2},{5,3},{6,0},{7,1},{8,14},{9,15},{10,... | collective-permute-start | bytes 196616 | tf_op jit(solution)/shard_map/ppermute | solution.py:87
  44.3 7.0 %collective-permute-start.8 = (bf16[1,128,256]{2,1,0:T(8,128)(2,1)S(1)}, bf16[1,128,256]{2,1,0:T(8,128)(2,1)S(1)}, u32[]{:S(2)}, u32[]{:S(2)}) collective-permute-start(bf16[1,128,256]{2,1,0:T(8,128)(2,1)S(1)} %copy-done.9), channel_id=1, source_target_pairs={{0,7},{1,6},{2,5},{3,4},{4,3},{5,2},{6,1},{7,0},{8,15},{9,14},{10,... | collective-permute-start | bytes 196616 | tf_op jit(solution)/shard_map/ppermute | solution.py:87
  51.3 0.7 copy-start.19
  52.0 1.7 copy-start.4
  53.8 1.0 copy-start.5
  53.8 1.0 copy-start.8
  56.1 2.4 %copy-start.17 = (pred[40]{0:T(512)(128)(4,1)S(1)}, pred[40]{0:T(512)(128)(4,1)}, u32[]{:S(2)}) copy-start(pred[40]{0:T(512)(128)(4,1)} %get-tuple-element.62) | copy-start | bytes 124
  68.2 3.4 %copy-start.16 = (pred[40]{0:T(512)(128)(4,1)S(1)}, pred[40]{0:T(512)(128)(4,1)}, u32[]{:S(2)}) copy-start(pred[40]{0:T(512)(128)(4,1)} %iota_compare_fusion.1) | copy-start | bytes 124
  71.6 2.5 %copy-start.1 = (bf16[40,128,256]{2,0,1:T(8,128)(2,1)S(1)}, bf16[40,128,256]{2,0,1:T(8,128)(2,1)}, u32[]{:S(2)}) copy-start(bf16[40,128,256]{2,0,1:T(8,128)(2,1)} %copy.23) | copy-start | bytes 7864324
  74.1 5.0 %copy-start.20 = (s32[256]{0:T(256)S(1)}, s32[256]{0:T(256)}, u32[]{:S(2)}) copy-start(s32[256]{0:T(256)} %scatter_custom_fusion.1) | copy-start | bytes 3076
  74.7 16.5 %copy-start.22 = (s32[1,8]{1,0:T(1,128)S(1)}, s32[1,8]{1,0:T(1,128)}, u32[]{:S(2)}) copy-start(s32[1,8]{1,0:T(1,128)} %param.29) | copy-start | bytes 100
  75.5 15.6 %all-to-all-start = ((bf16[8,128,256]{2,1,0:T(8,128)(2,1)}), bf16[8,128,256]{2,1,0:T(8,128)(2,1)S(1)}, u32[]{:S(2)}, u32[]{:S(2)}) async-start(bf16[8,128,256]{2,1,0:T(8,128)(2,1)} %copy.24), calls=%async_computation | async-start | bytes 1048576 | tf_op jit(solution)/shard_map/all_to_all | solution.py:128
  79.0 138.4 %all-reduce.2.cloned.1.call-start = ((), (), s32[]{:S(2)}) async-start(), calls=%async_computation.1 | async-start | bytes 524288 | tf_op jit(solution)/shard_map/psum | solution.py:139
  79.1 12.8 %copy-start.7 = (bf16[256,256]{1,0:T(8,128)(2,1)S(1)}, bf16[256,256]{1,0:T(8,128)(2,1)}, u32[]{:S(2)}) copy-start(bf16[256,256]{1,0:T(8,128)(2,1)} %copy-done.6) | copy-start | bytes 393220
  79.5 12.2 %collective-permute-start.10 = (bf16[256,256]{1,0:T(8,128)(2,1)S(1)}, bf16[256,256]{1,0:T(8,128)(2,1)S(1)}, u32[]{:S(2)}, u32[]{:S(2)}) collective-permute-start(bf16[256,256]{1,0:T(8,128)(2,1)S(1)} %get-tuple-element.55), channel_id=1, source_target_pairs={{8,0},{16,8},{24,16},{0,24},{9,1},{17,9},{25,17},{1,25},{10,2},{18... | collective-permute-start | bytes 393224 | tf_op jit(solution)/shard_map/ppermute | solution.py:18
  79.5 12.1 %collective-permute-start.9 = (bf16[256,256]{1,0:T(8,128)(2,1)S(1)}, bf16[256,256]{1,0:T(8,128)(2,1)S(1)}, u32[]{:S(2)}, u32[]{:S(2)}) collective-permute-start(bf16[256,256]{1,0:T(8,128)(2,1)S(1)} %get-tuple-element.54), channel_id=1, source_target_pairs={{0,8},{8,16},{16,24},{24,0},{1,9},{9,17},{17,25},{25,1},{2,10},{10... | collective-permute-start | bytes 393224 | tf_op jit(solution)/shard_map/ppermute | solution.py:16
Sparse Core Ops, SparseCore 0:
  94.2 123.1 all-reduce.1
